TPU v7x, 256 devices: a whole 4x4x8 slice. The times are simulated.
256 devices in a mesh: gx: 8 (over x, core), gy: 8 (over z), gz: 4 (over y).
Axes of the slice: x: 4, y: 4, z: 8, core: 2. Of those that a mesh axis runs over, the one named last changes fastest.
Arguments:
- flat_weight: float32 [6144, 128, 128], P(('gx', 'gy', 'gz')), may hold values from -6 to 6
- flat_first: float32 [6144, 128, 128], P(('gx', 'gy', 'gz')), may hold values from -3 to 3
- flat_second: float32 [6144, 128, 128], P(('gx', 'gy', 'gz')), may hold values from 0.01 to 1
- tile_map: int32 [6144], P(('gx', 'gy', 'gz')), may hold values from 0 to 6143, as said below
- tile_seeds: int32 [64, 96], P(('gx', 'gy'), 'gz'), may hold values from 0 to 16777215
- tokens: bfloat16 [3072, 12288], P(('gy', 'gx'), 'gz'), may hold values from -6 to 6
- grad_out: bfloat16 [3072, 8192], P('gy', ('gx', 'gz')), may hold values from -6 to 6
Outputs:
- outputs: bfloat16 [3072, 8192], P('gy', ('gx', 'gz'))
- input_grad: bfloat16 [3072, 12288], P(('gy', 'gx'), 'gz')
- weight_new: float32 [8192, 12288], P(('gx', 'gy'), 'gz')
- first_new: float32 [8192, 12288], P(('gx', 'gy'), 'gz')
- second_new: float32 [8192, 12288], P(('gx', 'gy'), 'gz')
Inputs may be any that keep to these rules, and one draw needn't show every extreme that they name: `tile_map`: every tile of the slab is held by exactly one slot. Device rank r = ((a * 8) + b) * 4 + c holds slots r * 24 onward; it holds only tiles of the block owned by some device with the same b, where the owner of rows 128 * R onward and columns 128 * C onward has a = R // 8, b = (R) % 8, c = C // 24. One device holds at most 2 tiles of one owner, and exactly 2 of some owner.
All inputs are finite; a program needn't handle non-finite values.
Results may differ from a plain program's by a relative error of at most 0.013.
Values may be sent and summed in bfloat16 or wider, within the bound.
No kernel may reach another device: no remote copies, remote signals or barrier semaphores. Data moves between devices by JAX's collectives and lax.ppermute only.
A program may use at most 128 MiB of HBM per device.

v0:
```python
import math
import jax
import jax.numpy as jnp
from jax import lax
from jax.sharding import PartitionSpec as P

D = 12288
BETA_ONE = 0.9
BETA_TWO = 0.95
LEARN_RATE = 0.01
WEIGHT_DECAY = 0.1
EPSILON = 1e-08
BIAS_ONE = 0.9999734386011125
BIAS_TWO = 0.994079470779666
DITHER_SCALE = 0.25


def dither(seeds, position):
    mixing = seeds + position * 1640531527
    mixing = mixing ^ mixing >> 15 & 131071
    mixing = mixing * 739982445
    mixing = mixing ^ mixing >> 12 & 1048575
    mixing = mixing * 695872825
    mixing = mixing ^ mixing >> 15 & 131071
    return (mixing & 65535).astype(jnp.float32) / 65536.0 - 0.5


def body(flat_weight, flat_first, flat_second, tile_map, tile_seeds, tokens, grad_out):
    size_gx = lax.axis_size("gx")
    size_gy = lax.axis_size("gy")
    size_gz = lax.axis_size("gz")
    group_size = size_gx * size_gz
    tiles_own = flat_weight.shape[0]
    tile_side = flat_weight.shape[1]
    row_tiles = tile_seeds.shape[0]
    col_tiles = tile_seeds.shape[1]
    capacity = max(2, (2 * tiles_own + group_size - 1) // group_size - 1)
    total_slots = group_size * capacity
    across = col_tiles * size_gz
    row_block = tile_map // across
    col_block = tile_map % across
    target = row_block // row_tiles // size_gy * size_gz + col_block // col_tiles
    local_tile = row_block % row_tiles * col_tiles + col_block % col_tiles
    ordinal = jnp.arange(tiles_own, dtype=jnp.int32)
    same_owner = (target[:, None] == target[None, :]) & (ordinal[None, :] < ordinal[:, None])
    ranking = jnp.sum(same_owner.astype(jnp.int32), axis=1)
    position = target * capacity + ranking
    slot_ids = jnp.arange(total_slots, dtype=jnp.int32)
    matches = (position[None, :] == slot_ids[:, None]).astype(jnp.int32)
    source = jnp.sum(matches * ordinal[None, :], axis=1)
    filled = jnp.sum(matches, axis=1).astype(jnp.float32)[:, None, None]
    labels = jnp.sum(matches * (local_tile[None, :] + 1), axis=1)
    grid_shape = (group_size, capacity, tile_side, tile_side)
    send_weight = (jnp.take(flat_weight, source, axis=0) * filled).astype(jnp.bfloat16)
    got_labels = lax.all_to_all(
        labels.reshape(group_size, capacity), ("gx", "gz"), split_axis=0, concat_axis=0, tiled=True
    )
    got_weight = lax.all_to_all(
        send_weight.reshape(grid_shape), ("gx", "gz"), split_axis=0, concat_axis=0, tiled=True
    )
    token_band = lax.all_gather(tokens, "gx", axis=0, tiled=True)
    got_weight, token_band = lax.optimization_barrier((got_weight, token_band))
    got_weight = got_weight.astype(jnp.float32)
    got_labels = got_labels.reshape(total_slots)
    wanted = jnp.arange(1, tiles_own + 1, dtype=jnp.int32)
    hits = (got_labels[None, :] == wanted[:, None]).astype(jnp.int32)
    picked = jnp.sum(hits * slot_ids[None, :], axis=1)

    def place(received):
        flat_tiles = jnp.take(received.reshape(total_slots, tile_side, tile_side), picked, axis=0)
        tile_grid = flat_tiles.reshape(row_tiles, col_tiles, tile_side, tile_side)
        return tile_grid.transpose(0, 2, 1, 3).reshape(row_tiles * tile_side, col_tiles * tile_side)

    weight = place(got_weight)
    weight_low = weight.astype(jnp.bfloat16)
    weight_band = lax.all_gather(weight_low, "gy", axis=0, tiled=True)
    send_moments = jnp.stack(
        [
            jnp.take(flat_first, source, axis=0) * filled,
            jnp.take(flat_second, source, axis=0) * filled,
        ],
        axis=1,
    ).astype(jnp.bfloat16)
    send_moments, weight_band = lax.optimization_barrier((send_moments, weight_band))
    got_moments = (
        lax.all_to_all(
            send_moments.reshape(group_size, capacity, 2, tile_side, tile_side),
            ("gx", "gz"),
            split_axis=0,
            concat_axis=0,
            tiled=True,
        )
        .astype(jnp.float32)
        .reshape(total_slots, 2, tile_side, tile_side)
    )
    first_moment = place(got_moments[:, 0])
    second_moment = place(got_moments[:, 1])
    factor = 1.0 / math.sqrt(D)
    partial_out = factor * jnp.dot(token_band, weight_band.T, preferred_element_type=jnp.float32)
    outputs = lax.psum_scatter(
        partial_out.astype(jnp.bfloat16), "gz", scatter_dimension=1, tiled=True
    )
    grad_band = lax.all_gather(grad_out.T, "gz", axis=0, tiled=True).T
    input_grad = lax.psum_scatter(
        (factor * jnp.dot(grad_band, weight_band, preferred_element_type=jnp.float32)).astype(
            jnp.bfloat16
        ),
        "gx",
        scatter_dimension=0,
        tiled=True,
    )
    gradient = lax.psum_scatter(
        (
            factor
            * lax.dot_general(
                grad_band, token_band, (((0,), (0,)), ((), ())), preferred_element_type=jnp.float32
            )
        ).astype(jnp.bfloat16),
        "gy",
        scatter_dimension=0,
        tiled=True,
    ).astype(jnp.float32)
    first_new = BETA_ONE * first_moment + (1.0 - BETA_ONE) * gradient
    second_new = BETA_TWO * second_moment + (1.0 - BETA_TWO) * gradient * gradient
    direction = (
        first_new / BIAS_ONE / (jnp.sqrt(second_new / BIAS_TWO) + EPSILON) + WEIGHT_DECAY * weight
    )
    moved = weight - LEARN_RATE * direction
    block_shape = weight.shape
    row_ids = lax.broadcasted_iota(jnp.int32, block_shape, 0)
    col_ids = lax.broadcasted_iota(jnp.int32, block_shape, 1)
    seed_full = jnp.repeat(jnp.repeat(tile_seeds, tile_side, axis=0), tile_side, axis=1)
    noise = dither(seed_full, row_ids % tile_side * tile_side + col_ids % tile_side)
    weight_new = moved + jnp.abs(moved) * DITHER_SCALE * noise
    return (outputs, input_grad, weight_new, first_new, second_new)


def solution(mesh):
    return jax.shard_map(
        body,
        mesh=mesh,
        in_specs=(
            P(("gx", "gy", "gz"), None, None),
            P(("gx", "gy", "gz"), None, None),
            P(("gx", "gy", "gz"), None, None),
            P(("gx", "gy", "gz")),
            P(("gx", "gy"), "gz"),
            P(("gy", "gx"), "gz"),
            P("gy", ("gx", "gz")),
        ),
        out_specs=(
            P("gy", ("gx", "gz")),
            P(("gy", "gx"), "gz"),
            P(("gx", "gy"), "gz"),
            P(("gx", "gy"), "gz"),
            P(("gx", "gy"), "gz"),
        ),
        check_vma=False,
    )
```

profile of v0, /device:TPU:8, one launch (start us, length us, event | category | flops | bytes accessed | tf_op | source)
XLA Modules:
  0.0 306.8 jit_solution(18281767544763607784)
XLA Ops:
  7.2 0.0 copy-start
  7.2 0.0 all-gather.3.cloned.1.call-start
  7.2 0.7 all-gather.3.cloned.1.call-update
  7.9 0.7 fusion.19
  8.6 0.2 convert_reduce_fusion.1
  8.8 0.1 select_reduce_fusion.1
  8.9 0.7 all_to_all.13
  9.6 7.5 %all-to-all-start.1 = ((s32[32,1,2]{2,1,0:T(1,128)}), s32[32,1,2]{2,1,0:T(1,128)S(1)}, u32[]{:S(2)}, u32[]{:S(2)}) async-start(s32[32,1,2]{2,1,0:T(1,128)} %bitcast.4), calls=%async_computation.1 | async-start | bytes 32768 | tf_op jit(solution)/shard_map/all_to_all | solution.py:55
  17.2 0.0 copy-done
  17.2 0.0 copy-start.2
  17.2 2.8 gather_fusion.1
  20.0 0.0 copy-done.2
  20.0 2.8 gather_fusion.2
  22.8 0.0 copy-done.3
  22.8 2.8 gather_fusion
  25.6 7.6 %fusion.5 = (bf16[64,1,128,128]{3,2,1,0:T(8,128)(2,1)}, bf16[64,1,128,128]{3,2,1,0:T(8,128)(2,1)}, bf16[64,128,128]{2,1,0:T(8,128)(2,1)}) fusion(f32[64,128,128]{2,1,0:T(8,128)} %gather_fusion.1, f32[64]{0:T(128)S(1)} %convert_element_type.46, pred[64]{0:T(512)(128)(4,1)S(1)} %compare_and_fusion.1, f32[64,128,128]{2,1,0:T(8,128)} %gather_fusion.2, ...), kind=kLoop, calls=%fused_computation.20 | loop fusion | flops 9437184 | bytes 18874688 | tf_op jit(solution)/shard_map/stack | solution.py:77
  33.2 0.0 all-to-all-done.1
  33.2 7.6 %all-to-all-start = ((bf16[32,2,128,128]{3,2,1,0:T(8,128)(2,1)}), bf16[32,2,128,128]{3,2,1,0:T(8,128)(2,1)}, u32[]{:S(2)}, u32[]{:S(2)}) async-start(bf16[32,2,128,128]{3,2,1,0:T(8,128)(2,1)} %bitcast.65), calls=%async_computation | async-start | bytes 4194304 | tf_op jit(solution)/shard_map/all_to_all | solution.py:58
  40.8 0.0 all-gather.5.cloned.1.call-start
  40.9 0.5 broadcast.207
  41.4 0.7 reduce.3
  42.1 0.1 eq.54
  42.2 0.2 select_reduce_fusion
  42.4 25.4 %all-to-all-done = bf16[32,2,128,128]{3,2,1,0:T(8,128)(2,1)} async-done(((bf16[32,2,128,128]{3,2,1,0:T(8,128)(2,1)}), bf16[32,2,128,128]{3,2,1,0:T(8,128)(2,1)}, u32[]{:S(2)}, u32[]{:S(2)}) %all-to-all-start) | async-done | bytes 2097184 | tf_op jit(solution)/shard_map/all_to_all | solution.py:58
  67.8 4.1 %bitcast_convert_fusion = f32[64,128,128]{2,1,0:T(8,128)} fusion(bf16[32,2,128,128]{3,2,1,0:T(8,128)(2,1)} %all-to-all-done), kind=kLoop, calls=%fused_computation.22 | loop fusion | flops 1048576 | bytes 6291456 | tf_op jit(solution)/shard_map/reshape | solution.py:70
  71.9 2.8 gather_fusion.3
  74.7 0.2 select_bitcast_fusion
  74.9 0.5 copy.42
  75.4 0.0 copy-start.5
  75.4 1.0 bitcast_convert_fusion.1
  76.3 0.0 all-gather.5.cloned.1.call-update
  76.4 0.0 reduce-scatter.12.cloned.1.call-start
  76.4 14.6 %all_gather.11 = bf16[1024,384]{0,1:T(8,128)(2,1)S(1)} all-gather(bf16[256,384]{0,1:T(8,128)(2,1)S(1)} %bitcast.66), channel_id=1, replica_groups=mesh['gx'=8,'gy'=8,'gz'=4] {'gz'}, dimensions={0}, use_global_device_ids=true | all-gather | bytes 983040 | tf_op jit(solution)/shard_map/all_gather | solution.py:103
  91.1 7.2 %fusion = bf16[1024,3072]{0,1:T(8,128)(2,1)} fusion(bf16[384,3072]{1,0:T(8,128)(2,1)} %all-gather.3.cloned.1.call-done, bf16[1024,384]{0,1:T(8,128)(2,1)S(1)} %all_gather.11), kind=kOutput, calls=%fused_computation.7 | convolution fusion | flops 2422210560 | bytes 9437184 | tf_op jit(solution)/shard_map/dot_general | solution.py:115
  98.2 8.6 %copy.53 = bf16[1024,3072]{1,0:T(8,128)(2,1)} copy(bf16[1024,3072]{0,1:T(8,128)(2,1)} %fusion) | data formatting | bytes 12582912
  106.9 0.0 reduce-scatter.12.cloned.1.call-update
  106.9 0.0 reduce-scatter.8.cloned.1.call-start
  107.0 4.6 %pad_maximum_fusion = bf16[64,2,128,128]{3,2,1,0:T(8,128)(2,1)} fusion(bf16[64,1,128,128]{3,2,1,0:T(8,128)(2,1)} %get-tuple-element.49, bf16[64,1,128,128]{3,2,1,0:T(8,128)(2,1)} %get-tuple-element.48), kind=kLoop, calls=%fused_computation.11 | loop fusion | flops 2097152 | bytes 8388608 | tf_op jit(solution)/shard_map/stack | solution.py:77
  111.5 46.1 %all-gather.5.cloned.1.call-done = bf16[1024,3072]{0,1:T(8,128)(2,1)} async-done(((bf16[128,3072]{0,1:T(8,128)(2,1)}), bf16[1024,3072]{0,1:T(8,128)(2,1)}) %all-gather.5.cloned.1.call-update) | async-done | bytes 6291472 | tf_op jit(solution)/shard_map/all_gather | solution.py:76
  157.7 7.0 %multiply_convert_fusion.2 = bf16[384,1024]{1,0:T(8,128)(2,1)} fusion(bf16[384,3072]{1,0:T(8,128)(2,1)} %all-gather.3.cloned.1.call-done, bf16[1024,3072]{0,1:T(8,128)(2,1)} %all-gather.5.cloned.1.call-done), kind=kOutput, calls=%fused_computation.37 | convolution fusion | flops 2416705536 | bytes 9437184 | tf_op jit(solution)/shard_map/dot_general | solution.py:99
  164.7 0.0 reduce-scatter.8.cloned.1.call-update
  164.7 4.7 %copy.43 = bf16[32,2,2,128,128]{4,3,1,2,0:T(8,128)(2,1)} copy(bf16[32,2,2,128,128]{4,3,2,1,0:T(8,128)(2,1)} %bitcast.64) | data formatting | bytes 8388608 | tf_op jit(solution)/shard_map/reshape | solution.py:87
  169.4 7.5 %all-to-all-start.2 = ((bf16[32,2,2,128,128]{4,3,1,2,0:T(8,128)(2,1)}), bf16[32,2,2,128,128]{4,3,1,2,0:T(8,128)(2,1)}, u32[]{:S(2)}, u32[]{:S(2)}) async-start(bf16[32,2,2,128,128]{4,3,1,2,0:T(8,128)(2,1)} %copy.43), calls=%async_computation.3 | async-start | bytes 8388608 | tf_op jit(solution)/shard_map/all_to_all | solution.py:86
  176.8 0.2 reduce-scatter.10.cloned.1.call-start
  177.1 7.7 %fusion.4 = bf16[384,3072]{0,1:T(8,128)(2,1)} fusion(bf16[1024,3072]{0,1:T(8,128)(2,1)} %all-gather.5.cloned.1.call-done, bf16[1024,384]{0,1:T(8,128)(2,1)S(1)} %all_gather.11), kind=kOutput, calls=%fused_computation.18 | convolution fusion | flops 2418278400 | bytes 9437184 | tf_op jit(solution)/shard_map/dot_general | solution.py:105
  184.8 4.3 %copy.51 = bf16[384,3072]{1,0:T(8,128)(2,1)} copy(bf16[384,3072]{0,1:T(8,128)(2,1)} %fusion.4) | data formatting | bytes 4718592
  189.1 0.0 reduce-scatter.10.cloned.1.call-update
  189.2 0.6 copy-done.6
  189.8 0.1 broadcast_bitcast_fusion
  189.8 43.8 %reduce-scatter.12.cloned.1.call-done = bf16[128,3072]{1,0:T(8,128)(2,1)} async-done(((bf16[1024,3072]{1,0:T(8,128)(2,1)}), bf16[128,3072]{1,0:T(8,128)(2,1)}) %reduce-scatter.12.cloned.1.call-update) | async-done | bytes 786448
  233.6 2.3 copy.54
  235.9 0.0 all-to-all-done.2
  235.9 3.2 %copy.44 = f32[32,2,2,128,128]{4,3,1,0,2:T(8,128)S(1)} copy(bf16[32,2,2,128,128]{4,3,1,2,0:T(8,128)(2,1)} %all-to-all-done.2) | data formatting | bytes 12582912 | tf_op jit(solution)/shard_map/reshape | solution.py:94
  239.2 3.8 %slice_bitcast_fusion = (f32[64,128,128]{2,1,0:T(8,128)}, f32[64,128,128]{2,1,0:T(8,128)}) fusion(f32[64,2,128,128]{3,2,0,1:T(8,128)S(1)} %bitcast.63), kind=kLoop, calls=%fused_computation.9 | loop fusion | bytes 16777216 | tf_op jit(solution)/shard_map/squeeze | solution.py:97
  243.0 4.0 %gather_fusion.5 = f32[24,128,128]{2,1,0:T(8,128)} fusion(f32[64,128,128]{2,1,0:T(8,128)} %get-tuple-element.46, s32[1024]{0:T(1024)S(1)} %pad_clamp_fusion), kind=kCustom, calls=%fused_computation.5.clone | custom fusion | bytes 3145824 | tf_op jit(solution)/shard_map/jit(_take)/gather | solution.py:70
  247.0 4.0 %gather_fusion.4 = f32[24,128,128]{2,1,0:T(8,128)} fusion(f32[64,128,128]{2,1,0:T(8,128)} %get-tuple-element.47, s32[1024]{0:T(1024)S(1)} %pad_clamp_fusion), kind=kCustom, calls=%fused_computation.4.clone | custom fusion | bytes 3145824 | tf_op jit(solution)/shard_map/jit(_take)/gather | solution.py:70
  250.9 3.6 %fusion.11 = (f32[1,128,24,128]{3,1,2,0:T(8,128)S(1)}, f32[1,128,24,128]{3,1,2,0:T(8,128)}) fusion(f32[24,128,128]{2,1,0:T(8,128)} %gather_fusion.5, pred[24]{0:T(512)(128)(4,1)S(1)} %compare_and_fusion, f32[24,128,128]{2,1,0:T(8,128)} %gather_fusion.4), kind=kLoop, calls=%fused_computation.32 | loop fusion | flops 1572864 | bytes 6291480 | tf_op jit(solution)/shard_map/mul | solution.py:124
  254.6 3.0 copy.45
  257.6 1.6 copy.46
  259.2 9.5 %multiply_add_fusion = (f32[128,3072]{0,1:T(8,128)}, f32[128,3072]{0,1:T(8,128)}, f32[128,3072]{0,1:T(8,128)S(1)}) fusion(f32[1,128,24,128]{1,3,2,0:T(8,128)S(1)} %copy.42, s32[3072]{0:T(1024)S(1)} %get-tuple-element.55, s32[3072]{0:T(1024)S(1)} %get-tuple-element.56, s32[128]{0:T(128)S(1)} %get-tuple-element.57, s32[128]{0:T(128)S(1)} %get-tuple-element.58, ...), kind=kLoop, calls=%fused_computation.36 | loop fusion | flops 15335424 | bytes 10264704 | tf_op jit(solution)/shard_map/add | solution.py:134
  268.7 3.1 %copy.48 = f32[128,3072]{1,0:T(8,128)} copy(f32[128,3072]{0,1:T(8,128)} %get-tuple-element.43) | data formatting | bytes 3145728
  271.9 1.6 copy.49
  273.5 1.6 copy.50
  275.1 25.1 %reduce-scatter.10.cloned.1.call-done = bf16[48,3072]{1,0:T(8,128)(2,1)} async-done(((bf16[384,3072]{1,0:T(8,128)(2,1)}), bf16[48,3072]{1,0:T(8,128)(2,1)}) %reduce-scatter.10.cloned.1.call-update) | async-done | bytes 294928
  (22 shorter events, 0.1 us)
Async XLA Ops:
  7.2 10.0 %copy-start = (f32[24,128,128]{2,1,0:T(8,128)S(1)}, f32[24,128,128]{2,1,0:T(8,128)}, u32[]{:S(2)}) copy-start(f32[24,128,128]{2,1,0:T(8,128)} %param.12) | copy-start | bytes 4718596
  7.2 60.6 %all-gather.3.cloned.1.call-start = ((), (), s32[]{:S(2)}) async-start(), calls=%async_computation.6 | async-start | bytes 2654208 | tf_op jit(solution)/shard_map/all_gather | solution.py:61
  9.6 23.6 %all-to-all-start.1 = ((s32[32,1,2]{2,1,0:T(1,128)}), s32[32,1,2]{2,1,0:T(1,128)S(1)}, u32[]{:S(2)}, u32[]{:S(2)}) async-start(s32[32,1,2]{2,1,0:T(1,128)} %bitcast.4), calls=%async_computation.1 | async-start | bytes 32768 | tf_op jit(solution)/shard_map/all_to_all | solution.py:55
  17.2 2.8 copy-start.2
  20.0 2.8 copy-start.3
  33.2 34.6 %all-to-all-start = ((bf16[32,2,128,128]{3,2,1,0:T(8,128)(2,1)}), bf16[32,2,128,128]{3,2,1,0:T(8,128)(2,1)}, u32[]{:S(2)}, u32[]{:S(2)}) async-start(bf16[32,2,128,128]{3,2,1,0:T(8,128)(2,1)} %bitcast.65), calls=%async_computation | async-start | bytes 4194304 | tf_op jit(solution)/shard_map/all_to_all | solution.py:58
  40.8 116.8 %all-gather.5.cloned.1.call-start = ((), (), s32[]{:S(2)}) async-start(), calls=%async_computation.7 | async-start | bytes 7077888 | tf_op jit(solution)/shard_map/all_gather | solution.py:76
  75.4 1.0 copy-start.5
  76.4 157.3 %reduce-scatter.12.cloned.1.call-start = ((), (), s32[]{:S(2)}) async-start(), calls=%async_computation.10 | async-start | bytes 7077888
  106.9 168.2 %reduce-scatter.8.cloned.1.call-start = ((), (), s32[]{:S(2)}) async-start(), calls=%async_computation.8 | async-start | bytes 983040 | tf_op jit(solution)/shard_map/reduce_scatter | solution.py:100
  169.4 66.5 %all-to-all-start.2 = ((bf16[32,2,2,128,128]{4,3,1,2,0:T(8,128)(2,1)}), bf16[32,2,2,128,128]{4,3,1,2,0:T(8,128)(2,1)}, u32[]{:S(2)}, u32[]{:S(2)}) async-start(bf16[32,2,2,128,128]{4,3,1,2,0:T(8,128)(2,1)} %copy.43), calls=%async_computation.3 | async-start | bytes 8388608 | tf_op jit(solution)/shard_map/all_to_all | solution.py:86
  176.8 123.4 %reduce-scatter.10.cloned.1.call-start = ((), (), s32[]{:S(2)}) async-start(), calls=%async_computation.9 | async-start | bytes 2654208
  189.1 0.7 copy-start.6
  268.7 3.1 %copy-start.4 = (f32[128,3072]{0,1:T(8,128)S(1)}, f32[128,3072]{0,1:T(8,128)}, u32[]{:S(2)}) copy-start(f32[128,3072]{0,1:T(8,128)} %get-tuple-element.44) | copy-start | bytes 4718596
  273.5 26.8 %copy-start.1 = (f32[24,128,128]{2,1,0:T(8,128)S(1)}, f32[24,128,128]{2,1,0:T(8,128)}, u32[]{:S(2)}) copy-start(f32[24,128,128]{2,1,0:T(8,128)} %param.12) | copy-start | bytes 4718596
Sparse Core Ops, SparseCore 0:
  9.8 30.9 all-gather.2
  76.5 81.1 all-gather.4
  160.2 73.3 reduce-scatter.11
  236.6 21.5 reduce-scatter.7
  261.2 39.0 reduce-scatter.9
where the time goes:
time: 308 us; the launch traced here: 307 us
  waiting for transfers between devices  141 us (46%)
  local copies, waits for them, and re-layouts  59.6 us (19%)
  other arithmetic  32.4 us (11%)
  starting transfers between devices  23 us (7%)
  matrix products  21.9 us (7%)
  blocking collectives  14.6 us (5%)
  between operations  14 us (5%)
    unnamed x7, waiting for transfers between devices  69.7 us
    all_gather x1, waiting for transfers between devices, body(): weight_band = lax.all_gather(weight_low, 'gy', axis=0, tiled=True)  46.1 us
    all_to_all x1, waiting for transfers between devices, body(): lax.all_to_all(send_weight.reshape(grid_shape), ('gx', 'gz'), split_axis=...  25.4 us
    unnamed x20, local copies, waits for them, and re-layouts  22.2 us
    all_gather x1, blocking collectives, body(): grad_band = lax.all_gather(grad_out.T, 'gz', axis=0, tiled=True).T  14.6 us
    another operation x2, other arithmetic, body(): jnp.stack([jnp.take(flat_first, source, axis=0) * filled, jnp.take(flat_s...  12.2 us
    gather x3, local copies, waits for them, and re-layouts, place(): jnp.take(received.reshape(total_slots, tile_side, tile_side), picked, axi...  10.8 us
    add x1, other arithmetic, body(): weight_new = moved + jnp.abs(moved) * DITHER_SCALE * noise  9.5 us
  transfers between devices with their start and end apart: 8, of which 4 were waited for; matrix products, arithmetic and copies ran while one was open for 34% of the time, Pallas kernels for 0%

commit v1 on v0

--- a/solution.py
+++ b/solution.py
@@ -100,7 +100,9 @@
     outputs = lax.psum_scatter(
         partial_out.astype(jnp.bfloat16), "gz", scatter_dimension=1, tiled=True
     )
-    grad_band = lax.all_gather(grad_out.T, "gz", axis=0, tiled=True).T
+    grad_band = jnp.concatenate(
+        lax.all_to_all(jnp.stack([grad_out.T] * lax.axis_size("gz")), "gz", 0, 0), axis=0
+    ).T
     input_grad = lax.psum_scatter(
         (factor * jnp.dot(grad_band, weight_band, preferred_element_type=jnp.float32)).astype(
             jnp.bfloat16

time: 308 us -> 308 us (level)
    all_to_all x0 -> x1, blocking collectives: none -> 15.4 us  [body(): lax.all_to_all(jnp.stack([grad_out.T] * lax.axis_size('gz')), 'gz', 0, 0)]
    all_gather x1 -> x0, blocking collectives: 14.6 us -> none  [body(): grad_band = lax.all_gather(grad_out.T, 'gz', axis=0, tiled=True).T]
    unnamed x20 -> x22, local copies, waits for them, and re-layouts: 22.2 us -> 22.2 us
  transfers between devices with their start and end apart: 8 -> 8, of which waited for: 4 -> 4; matrix products, arithmetic and copies ran while one was open for 34% -> 33% of each run, Pallas kernels for 0% -> 0%
where the time goes in v1:
time: 308 us; the launch traced here: 307 us
  waiting for transfers between devices  142 us (46%)
  local copies, waits for them, and re-layouts  59.9 us (19%)
  other arithmetic  32.4 us (11%)
  starting transfers between devices  23 us (7%)
  matrix products  20.2 us (7%)
  blocking collectives  15.4 us (5%)
  between operations  14 us (5%)
    unnamed x7, waiting for transfers between devices  69.7 us
    all_gather x1, waiting for transfers between devices, body(): weight_band = lax.all_gather(weight_low, 'gy', axis=0, tiled=True)  46.8 us
    all_to_all x1, waiting for transfers between devices, body(): lax.all_to_all(send_weight.reshape(grid_shape), ('gx', 'gz'), split_axis=...  25.4 us
    unnamed x22, local copies, waits for them, and re-layouts  22.2 us
    all_to_all x1, blocking collectives, body(): lax.all_to_all(jnp.stack([grad_out.T] * lax.axis_size('gz')), 'gz', 0, 0)  15.4 us
    another operation x2, other arithmetic, body(): jnp.stack([jnp.take(flat_first, source, axis=0) * filled, jnp.take(flat_s...  12.2 us
    gather x3, local copies, waits for them, and re-layouts, place(): jnp.take(received.reshape(total_slots, tile_side, tile_side), picked, axi...  10.8 us
    add x1, other arithmetic, body(): weight_new = moved + jnp.abs(moved) * DITHER_SCALE * noise  9.5 us
  transfers between devices with their start and end apart: 8, of which 4 were waited for; matrix products, arithmetic and copies ran while one was open for 33% of the time, Pallas kernels for 0%

profile of v1, /device:TPU:8, one launch (start us, length us, event | category | flops | bytes accessed | tf_op | source)
XLA Modules:
  0.0 306.7 jit_solution(17567527642429593352)
XLA Ops:
  7.2 0.0 copy-start
  7.2 0.0 all-gather.3.cloned.1.call-start
  7.2 0.7 all-gather.3.cloned.1.call-update
  7.9 0.7 fusion.19
  8.6 0.2 convert_reduce_fusion.1
  8.8 0.1 select_reduce_fusion.1
  8.9 0.7 all_to_all.16
  9.6 7.5 %all-to-all-start.1 = ((s32[32,1,2]{2,1,0:T(1,128)}), s32[32,1,2]{2,1,0:T(1,128)S(1)}, u32[]{:S(2)}, u32[]{:S(2)}) async-start(s32[32,1,2]{2,1,0:T(1,128)} %bitcast.4), calls=%async_computation.1 | async-start | bytes 32768 | tf_op jit(solution)/shard_map/all_to_all | solution.py:55
  17.2 0.0 copy-start.2
  17.2 2.8 gather_fusion.1
  20.0 0.0 copy-done.2
  20.0 2.8 gather_fusion.2
  22.8 2.8 gather_fusion
  25.5 7.6 %fusion.5 = (bf16[64,1,128,128]{3,2,1,0:T(8,128)(2,1)}, bf16[64,1,128,128]{3,2,1,0:T(8,128)(2,1)}, bf16[64,128,128]{2,1,0:T(8,128)(2,1)}) fusion(f32[64,128,128]{2,1,0:T(8,128)} %gather_fusion.1, f32[64]{0:T(128)S(1)} %convert_element_type.46, pred[64]{0:T(512)(128)(4,1)S(1)} %compare_and_fusion.1, f32[64,128,128]{2,1,0:T(8,128)} %gather_fusion.2, ...), kind=kLoop, calls=%fused_computation.20 | loop fusion | flops 9437184 | bytes 18874688 | tf_op jit(solution)/shard_map/stack | solution.py:77
  33.2 0.0 all-to-all-done.1
  33.2 7.6 %all-to-all-start = ((bf16[32,2,128,128]{3,2,1,0:T(8,128)(2,1)}), bf16[32,2,128,128]{3,2,1,0:T(8,128)(2,1)}, u32[]{:S(2)}, u32[]{:S(2)}) async-start(bf16[32,2,128,128]{3,2,1,0:T(8,128)(2,1)} %bitcast.66), calls=%async_computation | async-start | bytes 4194304 | tf_op jit(solution)/shard_map/all_to_all | solution.py:58
  40.8 0.0 all-gather.5.cloned.1.call-start
  40.9 0.5 broadcast.209
  41.4 0.7 reduce.3
  42.1 0.1 eq.54
  42.2 0.2 select_reduce_fusion
  42.4 25.4 %all-to-all-done = bf16[32,2,128,128]{3,2,1,0:T(8,128)(2,1)} async-done(((bf16[32,2,128,128]{3,2,1,0:T(8,128)(2,1)}), bf16[32,2,128,128]{3,2,1,0:T(8,128)(2,1)}, u32[]{:S(2)}, u32[]{:S(2)}) %all-to-all-start) | async-done | bytes 2097184 | tf_op jit(solution)/shard_map/all_to_all | solution.py:58
  67.8 4.1 %bitcast_convert_fusion = f32[64,128,128]{2,1,0:T(8,128)} fusion(bf16[32,2,128,128]{3,2,1,0:T(8,128)(2,1)} %all-to-all-done), kind=kLoop, calls=%fused_computation.22 | loop fusion | flops 1048576 | bytes 6291456 | tf_op jit(solution)/shard_map/reshape | solution.py:70
  71.9 2.8 gather_fusion.3
  74.7 0.2 select_bitcast_fusion
  74.9 0.5 copy.46
  75.4 0.0 copy-start.5
  75.4 1.0 bitcast_convert_fusion.1
  76.3 0.0 all-gather.5.cloned.1.call-update
  76.4 0.0 reduce-scatter.12.cloned.1.call-start
  76.4 0.2 copy.47
  76.6 0.1 stack.22
  76.7 15.4 %all_to_all.24 = bf16[4,256,384]{2,1,0:T(8,128)(2,1)S(1)} all-to-all(bf16[4,256,384]{2,1,0:T(8,128)(2,1)S(1)} %stack.22), channel_id=1, replica_groups=mesh['gx'=8,'gy'=8,'gz'=4] {'gz'}, dimensions={0} | all-to-all | bytes 1572864 | tf_op jit(solution)/shard_map/all_to_all | solution.py:104
  92.1 5.5 %fusion = bf16[1024,3072]{0,1:T(8,128)(2,1)} fusion(bf16[384,3072]{1,0:T(8,128)(2,1)S(1)} %copy-done.7, bf16[1024,384]{1,0:T(8,128)(2,1)S(1)} %bitcast.67), kind=kOutput, calls=%fused_computation.7 | convolution fusion | flops 2422210560 | bytes 9437184 | tf_op jit(solution)/shard_map/dot_general | solution.py:117
  97.6 8.6 %copy.58 = bf16[1024,3072]{1,0:T(8,128)(2,1)} copy(bf16[1024,3072]{0,1:T(8,128)(2,1)} %fusion) | data formatting | bytes 12582912
  106.2 0.0 reduce-scatter.12.cloned.1.call-update
  106.3 0.0 reduce-scatter.8.cloned.1.call-start
  106.3 4.6 %pad_maximum_fusion = bf16[64,2,128,128]{3,2,1,0:T(8,128)(2,1)} fusion(bf16[64,1,128,128]{3,2,1,0:T(8,128)(2,1)} %get-tuple-element.49, bf16[64,1,128,128]{3,2,1,0:T(8,128)(2,1)} %get-tuple-element.48), kind=kLoop, calls=%fused_computation.11 | loop fusion | flops 2097152 | bytes 8388608 | tf_op jit(solution)/shard_map/stack | solution.py:77
  110.9 46.8 %all-gather.5.cloned.1.call-done = bf16[1024,3072]{0,1:T(8,128)(2,1)} async-done(((bf16[128,3072]{0,1:T(8,128)(2,1)}), bf16[1024,3072]{0,1:T(8,128)(2,1)}) %all-gather.5.cloned.1.call-update) | async-done | bytes 6291472 | tf_op jit(solution)/shard_map/all_gather | solution.py:76
  157.7 7.0 %multiply_convert_fusion.2 = bf16[384,1024]{1,0:T(8,128)(2,1)} fusion(bf16[384,3072]{1,0:T(8,128)(2,1)} %all-gather.3.cloned.1.call-done, bf16[1024,3072]{0,1:T(8,128)(2,1)} %all-gather.5.cloned.1.call-done), kind=kOutput, calls=%fused_computation.37 | convolution fusion | flops 2416705536 | bytes 9437184 | tf_op jit(solution)/shard_map/dot_general | solution.py:99
  164.7 0.0 reduce-scatter.8.cloned.1.call-update
  164.7 4.7 %copy.48 = bf16[32,2,2,128,128]{4,3,1,2,0:T(8,128)(2,1)} copy(bf16[32,2,2,128,128]{4,3,2,1,0:T(8,128)(2,1)} %bitcast.65) | data formatting | bytes 8388608 | tf_op jit(solution)/shard_map/reshape | solution.py:87
  169.4 7.5 %all-to-all-start.3 = ((bf16[32,2,2,128,128]{4,3,1,2,0:T(8,128)(2,1)}), bf16[32,2,2,128,128]{4,3,1,2,0:T(8,128)(2,1)}, u32[]{:S(2)}, u32[]{:S(2)}) async-start(bf16[32,2,2,128,128]{4,3,1,2,0:T(8,128)(2,1)} %copy.48), calls=%async_computation.4 | async-start | bytes 8388608 | tf_op jit(solution)/shard_map/all_to_all | solution.py:86
  176.8 0.2 reduce-scatter.10.cloned.1.call-start
  177.1 7.7 %fusion.4 = bf16[384,3072]{0,1:T(8,128)(2,1)} fusion(bf16[1024,3072]{0,1:T(8,128)(2,1)} %all-gather.5.cloned.1.call-done, bf16[1024,384]{1,0:T(8,128)(2,1)S(1)} %bitcast.68), kind=kOutput, calls=%fused_computation.18 | convolution fusion | flops 2418278400 | bytes 9437184 | tf_op jit(solution)/shard_map/dot_general | solution.py:107
  184.8 4.3 %copy.56 = bf16[384,3072]{1,0:T(8,128)(2,1)} copy(bf16[384,3072]{0,1:T(8,128)(2,1)} %fusion.4) | data formatting | bytes 4718592
  189.1 0.0 reduce-scatter.10.cloned.1.call-update
  189.2 0.6 copy-done.6
  189.8 0.1 broadcast_bitcast_fusion
  189.8 43.8 %reduce-scatter.12.cloned.1.call-done = bf16[128,3072]{1,0:T(8,128)(2,1)} async-done(((bf16[1024,3072]{1,0:T(8,128)(2,1)}), bf16[128,3072]{1,0:T(8,128)(2,1)}) %reduce-scatter.12.cloned.1.call-update) | async-done | bytes 786448
  233.6 2.3 copy.59
  235.9 0.0 all-to-all-done.3
  235.9 3.2 %copy.49 = f32[32,2,2,128,128]{4,3,1,0,2:T(8,128)S(1)} copy(bf16[32,2,2,128,128]{4,3,1,2,0:T(8,128)(2,1)} %all-to-all-done.3) | data formatting | bytes 12582912 | tf_op jit(solution)/shard_map/reshape | solution.py:94
  239.1 3.8 %slice_bitcast_fusion = (f32[64,128,128]{2,1,0:T(8,128)}, f32[64,128,128]{2,1,0:T(8,128)}) fusion(f32[64,2,128,128]{3,2,0,1:T(8,128)S(1)} %bitcast.64), kind=kLoop, calls=%fused_computation.9 | loop fusion | bytes 16777216 | tf_op jit(solution)/shard_map/squeeze | solution.py:97
  243.0 4.0 %gather_fusion.5 = f32[24,128,128]{2,1,0:T(8,128)} fusion(f32[64,128,128]{2,1,0:T(8,128)} %get-tuple-element.46, s32[1024]{0:T(1024)S(1)} %pad_clamp_fusion), kind=kCustom, calls=%fused_computation.5.clone | custom fusion | bytes 3145824 | tf_op jit(solution)/shard_map/jit(_take)/gather | solution.py:70
  246.9 4.0 %gather_fusion.4 = f32[24,128,128]{2,1,0:T(8,128)} fusion(f32[64,128,128]{2,1,0:T(8,128)} %get-tuple-element.47, s32[1024]{0:T(1024)S(1)} %pad_clamp_fusion), kind=kCustom, calls=%fused_computation.4.clone | custom fusion | bytes 3145824 | tf_op jit(solution)/shard_map/jit(_take)/gather | solution.py:70
  250.9 3.6 %fusion.11 = (f32[1,128,24,128]{3,1,2,0:T(8,128)S(1)}, f32[1,128,24,128]{3,1,2,0:T(8,128)}) fusion(f32[24,128,128]{2,1,0:T(8,128)} %gather_fusion.5, pred[24]{0:T(512)(128)(4,1)S(1)} %compare_and_fusion, f32[24,128,128]{2,1,0:T(8,128)} %gather_fusion.4), kind=kLoop, calls=%fused_computation.32 | loop fusion | flops 1572864 | bytes 6291480 | tf_op jit(solution)/shard_map/mul | solution.py:126
  254.5 3.0 copy.50
  257.6 1.6 copy.51
  259.2 9.5 %multiply_add_fusion = (f32[128,3072]{0,1:T(8,128)}, f32[128,3072]{0,1:T(8,128)}, f32[128,3072]{0,1:T(8,128)S(1)}) fusion(f32[1,128,24,128]{1,3,2,0:T(8,128)S(1)} %copy.46, s32[3072]{0:T(1024)S(1)} %get-tuple-element.55, s32[3072]{0:T(1024)S(1)} %get-tuple-element.56, s32[128]{0:T(128)S(1)} %get-tuple-element.57, s32[128]{0:T(128)S(1)} %get-tuple-element.58, ...), kind=kLoop, calls=%fused_computation.36 | loop fusion | flops 15335424 | bytes 10264704 | tf_op jit(solution)/shard_map/add | solution.py:136
  268.7 3.1 %copy.53 = f32[128,3072]{1,0:T(8,128)} copy(f32[128,3072]{0,1:T(8,128)} %get-tuple-element.43) | data formatting | bytes 3145728
  271.8 1.6 copy.54
  273.5 1.6 copy.55
  275.1 25.1 %reduce-scatter.10.cloned.1.call-done = bf16[48,3072]{1,0:T(8,128)(2,1)} async-done(((bf16[384,3072]{1,0:T(8,128)(2,1)}), bf16[48,3072]{1,0:T(8,128)(2,1)}) %reduce-scatter.10.cloned.1.call-update) | async-done | bytes 294928
  (26 shorter events, 0.1 us)
Async XLA Ops:
  7.2 10.0 %copy-start = (f32[24,128,128]{2,1,0:T(8,128)S(1)}, f32[24,128,128]{2,1,0:T(8,128)}, u32[]{:S(2)}) copy-start(f32[24,128,128]{2,1,0:T(8,128)} %param.12) | copy-start | bytes 4718596
  7.2 60.6 %all-gather.3.cloned.1.call-start = ((), (), s32[]{:S(2)}) async-start(), calls=%async_computation.7 | async-start | bytes 2654208 | tf_op jit(solution)/shard_map/all_gather | solution.py:61
  9.6 23.6 %all-to-all-start.1 = ((s32[32,1,2]{2,1,0:T(1,128)}), s32[32,1,2]{2,1,0:T(1,128)S(1)}, u32[]{:S(2)}, u32[]{:S(2)}) async-start(s32[32,1,2]{2,1,0:T(1,128)} %bitcast.4), calls=%async_computation.1 | async-start | bytes 32768 | tf_op jit(solution)/shard_map/all_to_all | solution.py:55
  17.2 2.8 copy-start.2
  20.0 2.8 copy-start.3
  33.2 34.6 %all-to-all-start = ((bf16[32,2,128,128]{3,2,1,0:T(8,128)(2,1)}), bf16[32,2,128,128]{3,2,1,0:T(8,128)(2,1)}, u32[]{:S(2)}, u32[]{:S(2)}) async-start(bf16[32,2,128,128]{3,2,1,0:T(8,128)(2,1)} %bitcast.66), calls=%async_computation | async-start | bytes 4194304 | tf_op jit(solution)/shard_map/all_to_all | solution.py:58
  40.8 116.8 %all-gather.5.cloned.1.call-start = ((), (), s32[]{:S(2)}) async-start(), calls=%async_computation.8 | async-start | bytes 7077888 | tf_op jit(solution)/shard_map/all_gather | solution.py:76
  75.4 1.0 copy-start.5
  76.4 157.2 %reduce-scatter.12.cloned.1.call-start = ((), (), s32[]{:S(2)}) async-start(), calls=%async_computation.11 | async-start | bytes 7077888
  76.6 15.5 %copy-start.7 = (bf16[384,3072]{1,0:T(8,128)(2,1)S(1)}, bf16[384,3072]{1,0:T(8,128)(2,1)}, u32[]{:S(2)}) copy-start(bf16[384,3072]{1,0:T(8,128)(2,1)} %all-gather.3.cloned.1.call-done) | copy-start | bytes 7077892
  106.3 168.8 %reduce-scatter.8.cloned.1.call-start = ((), (), s32[]{:S(2)}) async-start(), calls=%async_computation.9 | async-start | bytes 983040 | tf_op jit(solution)/shard_map/reduce_scatter | solution.py:100
  169.4 66.5 %all-to-all-start.3 = ((bf16[32,2,2,128,128]{4,3,1,2,0:T(8,128)(2,1)}), bf16[32,2,2,128,128]{4,3,1,2,0:T(8,128)(2,1)}, u32[]{:S(2)}, u32[]{:S(2)}) async-start(bf16[32,2,2,128,128]{4,3,1,2,0:T(8,128)(2,1)} %copy.48), calls=%async_computation.4 | async-start | bytes 8388608 | tf_op jit(solution)/shard_map/all_to_all | solution.py:86
  176.8 123.4 %reduce-scatter.10.cloned.1.call-start = ((), (), s32[]{:S(2)}) async-start(), calls=%async_computation.10 | async-start | bytes 2654208
  189.1 0.7 copy-start.6
  268.7 3.1 %copy-start.4 = (f32[128,3072]{0,1:T(8,128)S(1)}, f32[128,3072]{0,1:T(8,128)}, u32[]{:S(2)}) copy-start(f32[128,3072]{0,1:T(8,128)} %get-tuple-element.44) | copy-start | bytes 4718596
  273.5 26.7 %copy-start.1 = (f32[24,128,128]{2,1,0:T(8,128)S(1)}, f32[24,128,128]{2,1,0:T(8,128)}, u32[]{:S(2)}) copy-start(f32[24,128,128]{2,1,0:T(8,128)} %param.12) | copy-start | bytes 4718596
Sparse Core Ops, SparseCore 0:
  9.8 30.9 all-gather.2
  76.5 81.1 all-gather.4
  160.2 73.3 reduce-scatter.11
  236.6 21.4 reduce-scatter.7
  261.1 39.0 reduce-scatter.9
